TPU v7x, 128 devices: a whole 4x4x4 slice. The times are simulated.
128 devices in a mesh: kv: 4 (over x), tok: 32 (over z, y, core).
Axes of the slice: x: 4, y: 4, z: 4, core: 2. Of those that a mesh axis runs over, the one named last changes fastest.
Arguments:
- dec_tokens: bfloat16 [512, 5120], P('tok', 'kv'), may hold values from -60 to 60
- pre_tokens: bfloat16 [8192, 5120], P('tok', 'kv'), may hold values from -60 to 60
- w_query: bfloat16 [5120, 2560], P(None, 'kv'), may hold values from -0.078125 to 0.078125
- w_keyval: bfloat16 [5120, 2, 512], P(None, None, 'kv'), may hold values from -0.078125 to 0.078125
- b_query: float32 [2560], P('kv'), may hold values from -3 to 3
- b_keyval: float32 [2, 512], P(None, 'kv'), may hold values from -3 to 3
- dec_pool: bfloat16 [2, 393216, 512], P(None, 'tok', 'kv'), may hold values from -72 to 72
- owner_slots: int32 [512], P('tok'), may hold values from 0 to 511, each once
- dec_lengths: int32 [512], P('tok'), may hold values from 1 to 4096, as said below
- pre_cache: bfloat16 [2, 32768, 512], P(None, 'tok', 'kv'), may hold values from -72 to 72
- pre_offsets: int32 [16], replicated, may hold values from 1536 to 2048
Outputs:
- dec_attn: bfloat16 [512, 2560], P('tok', 'kv')
- pre_attn: bfloat16 [8192, 2560], P('tok', 'kv')
- new_pool: bfloat16 [2, 393216, 512], P(None, 'tok', 'kv')
- pre_keyval: bfloat16 [2, 8192, 512], P(None, 'tok', 'kv')
Inputs may be any that keep to these rules, and one draw needn't show every extreme that they name: `dec_lengths`: in the 16 slots of each owner, one length is 512 or more and the others are below 512, so an owner's lengths plus one each sum to at most 12288.
All inputs are finite; a program needn't handle non-finite values.
Results may differ from a plain program's by a relative error of at most 0.0065.
The roundings to bfloat16 on the way count: a program that leaves them out, or rounds other values in their place, can miss the bound.
Values may be sent and summed in bfloat16 or wider, within the bound.
No kernel may reach another device: no remote copies, remote signals or barrier semaphores. Data moves between devices by JAX's collectives and lax.ppermute only.
A program may use at most 128 MiB of HBM per device.

v0:
```python
import jax
import jax.numpy as jnp
from jax import lax
from jax.sharding import PartitionSpec as P

HD = 128
THETA = 1000000.0


def swapped(value, axis, distance):
    return lax.ppermute(value, axis, [(i, i ^ 1 << distance) for i in range(lax.axis_size(axis))])


def rotate(values, positions):
    halfway = values.shape[-1] // 2
    spread = jnp.arange(halfway, dtype=jnp.float32) * (2.0 / values.shape[-1])
    rates = jnp.power(jnp.float32(THETA), -spread)
    angles = positions.astype(jnp.float32)[:, None] * rates[None, :]
    cosine = jnp.cos(angles)[:, None, :]
    sine = jnp.sin(angles)[:, None, :]
    former = values[..., :halfway]
    latter = values[..., halfway:]
    return jnp.concatenate(
        [former * cosine - latter * sine, latter * cosine + former * sine], axis=-1
    )


def head_scores(queries, key_rows, allowed):
    amount = queries.shape[0]
    q_heads = queries.shape[1] // HD
    shaped = queries.reshape(amount, q_heads, HD)
    product = jnp.einsum("ngd,md->ngm", shaped, key_rows, preferred_element_type=jnp.float32)
    scores = product * HD ** (-0.5)
    return jnp.where(allowed[:, None, :], scores, -jnp.inf)


def head_mix(scores, peaks, value_rows):
    powers = jnp.exp(scores - peaks[..., None])
    totals = jnp.sum(powers, axis=-1)
    weights = powers.astype(jnp.bfloat16)
    product = jnp.einsum("ngm,md->ngd", weights, value_rows, preferred_element_type=jnp.float32)
    return (totals, product)


def serve_owner(queries, keyval, lengths, cache_pool):
    amount = queries.shape[0]
    q_heads = queries.shape[1] // HD
    kv_heads = cache_pool.shape[2] // HD
    finish = jnp.cumsum(lengths + 1)
    starts = finish - lengths - 1
    turned = rotate(queries.astype(jnp.float32).reshape(amount, q_heads, HD), lengths)
    turned = turned.astype(jnp.bfloat16).reshape(amount, q_heads * HD)
    new_keys = rotate(keyval[:, 0].astype(jnp.float32).reshape(amount, kv_heads, HD), lengths)
    new_keys = new_keys.astype(jnp.bfloat16).reshape(amount, kv_heads * HD)
    appended = jnp.stack([new_keys, keyval[:, 1]], axis=0)
    cache_pool = cache_pool.at[:, starts + lengths].set(appended)
    spots = jnp.arange(cache_pool.shape[1], dtype=jnp.int32)
    allowed = (spots[None, :] >= starts[:, None]) & (spots[None, :] <= (starts + lengths)[:, None])
    scores = head_scores(turned, cache_pool[0], allowed)
    totals, mixed = head_mix(scores, jnp.max(scores, axis=-1), cache_pool[1])
    result = (mixed / totals[..., None]).astype(jnp.bfloat16).reshape(amount, q_heads * HD)
    return (result, cache_pool)


def tree_gather(value):
    place = lax.axis_index("tok")
    buffer = value
    for stride, count in ((1, 2), (2, 4), (8, 4)):
        parts = [buffer]
        for shift in range(1, count):
            pairs = []
            for i in range(32):
                digit = i // stride % count
                target = i + ((digit + shift) % count - digit) * stride
                pairs.append((i, target))
            parts.append(lax.ppermute(buffer, "tok", pairs))
        buffer = jnp.concatenate(parts, axis=0)
    return buffer


def tree_row(place, source, rows):
    core = place % 2 ^ source % 2
    y = (place // 2 % 4 - source // 2 % 4) % 4
    z = (place // 8 - source // 8) % 4
    return ((z * 4 + y) * 2 + core) * rows


def project(rows, w_query, kv_weight, b_query, kv_bias):
    cols = lax.all_gather(rows, "kv", axis=1, tiled=True)
    query = jnp.dot(cols, w_query, preferred_element_type=jnp.float32) + b_query
    keyval = jnp.dot(cols, kv_weight, preferred_element_type=jnp.float32) + kv_bias
    return (query, keyval)


def body(
    dec_tokens,
    pre_tokens,
    w_query,
    w_keyval,
    b_query,
    b_keyval,
    dec_pool,
    owner_slots,
    dec_lengths,
    pre_cache,
    pre_offsets,
):
    dec_count = dec_tokens.shape[0]
    pre_count = pre_tokens.shape[0]
    q_width = w_query.shape[1]
    kv_width = w_keyval.shape[2]
    kv_weight = w_keyval.reshape(w_keyval.shape[0], 2 * kv_width)
    kv_bias = b_keyval.reshape(2 * kv_width)
    dec_q, dec_kv = project(dec_tokens, w_query, kv_weight, b_query, kv_bias)
    tok_place = lax.axis_index("tok")
    ids = jnp.stack([owner_slots // dec_count, owner_slots % dec_count], axis=1).astype(
        jnp.bfloat16
    )
    used = q_width + 2 * kv_width + 2
    pad = jnp.zeros((dec_count, -(-used // 128) * 128 - used), jnp.bfloat16)
    sent = jnp.concatenate(
        [dec_q.astype(jnp.bfloat16), dec_kv.astype(jnp.bfloat16), ids, pad], axis=1
    )
    got = tree_gather(sent)
    rows = tree_row(tok_place, owner_slots // dec_count, dec_count) + owner_slots % dec_count
    chosen = jnp.take(got, rows, axis=0)
    dec_query = chosen[:, :q_width]
    dec_keyval = chosen[:, q_width : q_width + 2 * kv_width].reshape(dec_count, 2, kv_width)
    served, new_pool = serve_owner(dec_query, dec_keyval, dec_lengths, dec_pool)
    back = tree_gather(served)
    got_ids = got[:, q_width + 2 * kv_width : used].astype(jnp.int32)
    requests = got_ids[:, 0] * dec_count + got_ids[:, 1]
    wanted = tok_place * dec_count + jnp.arange(dec_count, dtype=jnp.int32)
    where = jnp.argmax(requests[None, :] == wanted[:, None], axis=1)
    dec_attn = jnp.take(back, where, axis=0)
    all_query, all_keyval = project(pre_tokens, w_query, kv_weight, b_query, kv_bias)
    half_id = tok_place % 2
    offset = pre_offsets[tok_place // 2]
    local_pos = jnp.arange(pre_count, dtype=jnp.int32)
    positions = offset + half_id * pre_count + local_pos
    q_heads = q_width // HD
    kv_heads = kv_width // HD
    turned = rotate(all_query.reshape(pre_count, q_heads, HD), positions)
    turned = turned.astype(jnp.bfloat16).reshape(pre_count, q_width)
    pre_kv = all_keyval.reshape(pre_count, 2, kv_width)
    new_keys = rotate(pre_kv[:, 0].reshape(pre_count, kv_heads, HD), positions)
    new_keys = new_keys.astype(jnp.bfloat16).reshape(pre_count, kv_width)
    appended = jnp.stack([new_keys, pre_kv[:, 1].astype(jnp.bfloat16)], axis=0)
    shard = pre_cache.shape[1]
    other_cache, other_new = swapped((pre_cache, appended), "tok", 0)
    is_lower = half_id == 0
    history = jnp.where(
        is_lower,
        jnp.concatenate([pre_cache, other_cache], axis=1),
        jnp.concatenate([other_cache, pre_cache], axis=1),
    )
    block_rows = jnp.where(
        is_lower,
        jnp.concatenate([appended, other_new], axis=1),
        jnp.concatenate([other_new, appended], axis=1),
    )
    key_rows = jnp.concatenate([history, block_rows], axis=1)
    key_slots = jnp.arange(key_rows.shape[1], dtype=jnp.int32)
    key_pos = jnp.where(key_slots < 2 * shard, key_slots, offset + key_slots - 2 * shard)
    usable = (key_slots < offset) | (key_slots >= 2 * shard)
    allowed = usable[None, :] & (key_pos[None, :] <= positions[:, None])
    scores = head_scores(turned, key_rows[0], allowed)
    totals, mixed = head_mix(scores, jnp.max(scores, axis=-1), key_rows[1])
    pre_attn = (mixed / totals[..., None]).astype(jnp.bfloat16).reshape(pre_count, q_width)
    return (dec_attn, pre_attn, new_pool, appended)


def solution(mesh):
    in_specs = (
        P("tok", "kv"),
        P("tok", "kv"),
        P(None, "kv"),
        P(None, None, "kv"),
        P("kv"),
        P(None, "kv"),
        P(None, "tok", "kv"),
        P("tok"),
        P("tok"),
        P(None, "tok", "kv"),
        P(),
    )
    out_specs = (P("tok", "kv"), P("tok", "kv"), P(None, "tok", "kv"), P(None, "tok", "kv"))
    return jax.shard_map(body, mesh=mesh, in_specs=in_specs, out_specs=out_specs, check_vma=False)
```

profile of v0, /device:TPU:1, one launch (start us, length us, event | category | flops | bytes accessed | tf_op | source)
XLA Modules:
  0.0 154.6 jit_solution(9778527914307117133)
XLA Ops:
  7.3 6.7 %copy.126 = bf16[2,12288,128]{2,1,0:T(8,128)(2,1)} copy(bf16[2,12288,128]{2,1,0:T(8,128)(2,1)} %param.17) | data formatting | bytes 12582912
  14.0 1.5 collective-permute-start.14
  16.3 9.8 %all_gather.6 = bf16[16,5120]{1,0:T(8,128)(2,1)S(1)} all-gather(bf16[16,1280]{1,0:T(8,128)(2,1)S(1)} %copy-done.5), channel_id=1, replica_groups=mesh['kv'=4,'tok'=32] {'kv'}, dimensions={1}, use_global_device_ids=true | all-gather | bytes 204800 | tf_op jit(solution)/shard_map/all_gather | solution.py:89
  26.6 4.2 %fusion.21 = bf16[16,640]{1,0:T(8,128)(2,1)S(1)} fusion(bf16[16,5120]{1,0:T(8,128)(2,1)S(1)} %all_gather.6, bf16[5120,640]{1,0:T(8,128)(2,1)} %param.13, f32[640]{0:T(1024)S(1)} %copy-done.8), kind=kOutput, calls=%fused_computation.31 | convolution fusion | flops 104878080 | bytes 6740480 | tf_op jit(solution)/shard_map/dot_general | solution.py:90
  30.9 2.3 %collective-permute-start = (bf16[16,1024]{1,0:T(8,128)(2,1)S(1)}, bf16[16,1024]{1,0:T(8,128)(2,1)S(1)}, u32[]{:S(2)}, u32[]{:S(2)}) collective-permute-start(bf16[16,1024]{1,0:T(8,128)(2,1)S(1)} %concatenate.83), channel_id=1, source_target_pairs={{0,1},{1,0},{2,3},{3,2},{4,5},{5,4},{6,7},{7,6},{8,9},{9,8},{10,11... | collective-permute-start | bytes 98312 | tf_op jit(solution)/shard_map/ppermute | solution.py:76
  37.8 1.3 multiply_cosine_fusion.1
  39.3 1.2 compare_and_fusion
  41.2 1.4 collective-permute-start.1
  42.5 2.6 %collective-permute-start.2 = (bf16[32,1024]{1,0:T(8,128)(2,1)S(1)}, bf16[32,1024]{1,0:T(8,128)(2,1)S(1)}, u32[]{:S(2)}, u32[]{:S(2)}) collective-permute-start(bf16[32,1024]{1,0:T(8,128)(2,1)S(1)} %pad_maximum_fusion.2), channel_id=1, source_target_pairs={{0,4},{1,5},{2,6},{3,7},{4,0},{5,1},{6,2},{7,3},{8,12},{9,13},{10,... | collective-permute-start | bytes 196616 | tf_op jit(solution)/shard_map/ppermute | solution.py:76
  47.5 1.2 collective-permute-done.2
  50.0 1.6 %collective-permute-start.4 = (bf16[128,1024]{1,0:T(8,128)(2,1)}, bf16[128,1024]{1,0:T(8,128)(2,1)}, u32[]{:S(2)}, u32[]{:S(2)}) collective-permute-start(bf16[128,1024]{1,0:T(8,128)(2,1)} %get-tuple-element.36), channel_id=1, source_target_pairs={{0,8},{1,9},{2,10},{3,11},{4,12},{5,13},{6,14},{7,15},{8,16},{9,17... | collective-permute-start | bytes 786440 | tf_op jit(solution)/shard_map/ppermute | solution.py:76
  52.4 3.4 %collective-permute-start.5 = (bf16[128,1024]{1,0:T(8,128)(2,1)}, bf16[128,1024]{1,0:T(8,128)(2,1)}, u32[]{:S(2)}, u32[]{:S(2)}) collective-permute-start(bf16[128,1024]{1,0:T(8,128)(2,1)} %get-tuple-element.36), channel_id=1, source_target_pairs={{0,16},{1,17},{2,18},{3,19},{4,20},{5,21},{6,22},{7,23},{8,24},{9,... | collective-permute-start | bytes 786440 | tf_op jit(solution)/shard_map/ppermute | solution.py:76
  57.8 2.1 %collective-permute-done.4 = bf16[128,1024]{1,0:T(8,128)(2,1)} collective-permute-done((bf16[128,1024]{1,0:T(8,128)(2,1)}, bf16[128,1024]{1,0:T(8,128)(2,1)}, u32[]{:S(2)}, u32[]{:S(2)}) %collective-permute-start.4) | collective-permute-done | bytes 262176 | tf_op jit(solution)/shard_map/ppermute | solution.py:76
  59.9 1.7 %constant_dynamic-update-slice_fusion.7 = bf16[512,1024]{1,0:T(8,128)(2,1)} fusion(bf16[512,1024]{1,0:T(8,128)(2,1)} %get-tuple-element.37, bf16[128,1024]{1,0:T(8,128)(2,1)} %collective-permute-done.4), kind=kLoop, calls=%fused_computation.83 | loop fusion | bytes 524288
  61.5 4.8 %collective-permute-done.5 = bf16[128,1024]{1,0:T(8,128)(2,1)} collective-permute-done((bf16[128,1024]{1,0:T(8,128)(2,1)}, bf16[128,1024]{1,0:T(8,128)(2,1)}, u32[]{:S(2)}, u32[]{:S(2)}) %collective-permute-start.5) | collective-permute-done | bytes 262176 | tf_op jit(solution)/shard_map/ppermute | solution.py:76
  66.4 1.7 %constant_dynamic-update-slice_fusion.6 = bf16[512,1024]{1,0:T(8,128)(2,1)} fusion(bf16[512,1024]{1,0:T(8,128)(2,1)} %constant_dynamic-update-slice_fusion.7, bf16[128,1024]{1,0:T(8,128)(2,1)} %collective-permute-done.5), kind=kLoop, calls=%fused_computation.82 | loop fusion | bytes 524288
  68.1 1.7 %constant_dynamic-update-slice_fusion.5 = bf16[512,1024]{1,0:T(8,128)(2,1)} fusion(bf16[512,1024]{1,0:T(8,128)(2,1)} %constant_dynamic-update-slice_fusion.6, bf16[128,1024]{1,0:T(8,128)(2,1)} %collective-permute-done.6), kind=kLoop, calls=%fused_computation.81 | loop fusion | bytes 524288 | tf_op jit(solution)/shard_map/concatenate | solution.py:77
  69.7 2.0 %gather_fusion = bf16[16,1024]{1,0:T(8,128)(2,1)S(1)} fusion(bf16[512,1024]{1,0:T(8,128)(2,1)} %constant_dynamic-update-slice_fusion.5, s32[1024]{0:T(1024)S(1)} %pad_clamp_fusion.1), kind=kCustom, calls=%fused_computation | custom fusion | bytes 65600 | tf_op jit(solution)/shard_map/jit(_take)/gather | solution.py:126
  76.8 2.4 %scatter_fusion = bf16[2,12288,128]{2,1,0:T(8,128)(2,1)} fusion(bf16[2,12288,128]{2,1,0:T(8,128)(2,1)} %copy.126, s32[16]{0:T(128)} %get-tuple-element.22, bf16[16,2,128]{2,0,1:T(8,128)(2,1)S(1)} %maximum_bitcast_fusion), kind=kCustom, calls=%fused_computation.2 | custom fusion | bytes 24640 | tf_op jit(solution)/shard_map/scatter | solution.py:56
  80.3 3.5 %fusion.100 = (f32[16,5]{0,1:T(8,128)S(1)}, f32[16,5,12288]{2,0,1:T(8,128)S(1)}) fusion(bf16[2,12288,128]{2,1,0:T(8,128)(2,1)} %scatter_fusion, bf16[16,5,64]{2,0,1:T(8,128)(2,1)S(1)} %get-tuple-element.33, bf16[16,5,64]{2,0,1:T(8,128)(2,1)S(1)} %get-tuple-element.32, pred[16,12288]{1,0:T(8,128)(4,1)S(1)} %fusion.43), kind=kOutput, calls=%fused_computation.192 | convolution fusion | flops 254648240 | bytes 7295296 | tf_op jit(solution)/shard_map/ngd,md->ngm/dot_general | solution.py:32
  85.5 1.8 %collective-permute-start.7 = (bf16[16,640]{1,0:T(8,128)(2,1)S(1)}, bf16[16,640]{1,0:T(8,128)(2,1)S(1)}, u32[]{:S(2)}, u32[]{:S(2)}) collective-permute-start(bf16[16,640]{1,0:T(8,128)(2,1)S(1)} %bitcast.93), channel_id=1, source_target_pairs={{0,1},{1,0},{2,3},{3,2},{4,5},{5,4},{6,7},{7,6},{8,9},{9,8},{10,11... | collective-permute-start | bytes 61448 | tf_op jit(solution)/shard_map/ppermute | solution.py:76
  90.6 2.6 %collective-permute-start.9 = (bf16[32,640]{1,0:T(8,128)(2,1)S(1)}, bf16[32,640]{1,0:T(8,128)(2,1)S(1)}, u32[]{:S(2)}, u32[]{:S(2)}) collective-permute-start(bf16[32,640]{1,0:T(8,128)(2,1)S(1)} %get-tuple-element.54), channel_id=1, source_target_pairs={{0,4},{1,5},{2,6},{3,7},{4,0},{5,1},{6,2},{7,3},{8,12},{9,13},{10,... | collective-permute-start | bytes 122888 | tf_op jit(solution)/shard_map/ppermute | solution.py:76
  97.4 1.7 %collective-permute-start.12 = (bf16[128,640]{1,0:T(8,128)(2,1)S(1)}, bf16[128,640]{1,0:T(8,128)(2,1)S(1)}, u32[]{:S(2)}, u32[]{:S(2)}) collective-permute-start(bf16[128,640]{1,0:T(8,128)(2,1)S(1)} %get-tuple-element.42), channel_id=1, source_target_pairs={{0,16},{1,17},{2,18},{3,19},{4,20},{5,21},{6,22},{7,23},{8,24},{9,... | collective-permute-start | bytes 491528 | tf_op jit(solution)/shard_map/ppermute | solution.py:76
  99.1 1.7 %collective-permute-start.13 = (bf16[128,640]{1,0:T(8,128)(2,1)S(1)}, bf16[128,640]{1,0:T(8,128)(2,1)S(1)}, u32[]{:S(2)}, u32[]{:S(2)}) collective-permute-start(bf16[128,640]{1,0:T(8,128)(2,1)S(1)} %get-tuple-element.42), channel_id=1, source_target_pairs={{0,24},{1,25},{2,26},{3,27},{4,28},{5,29},{6,30},{7,31},{8,0},{9,1... | collective-permute-start | bytes 491528 | tf_op jit(solution)/shard_map/ppermute | solution.py:76
  100.8 2.8 %maximum_select_fusion = bf16[2,2048,128]{2,1,0:T(8,128)(2,1)} fusion(bf16[2,1024,128]{2,1,0:T(8,128)(2,1)} %collective-permute-done.14, bf16[2,1024,128]{2,1,0:T(8,128)(2,1)} %param.20, pred[]{:T(512)S(6)} %eq.32), kind=kLoop, calls=%fused_computation.37 | loop fusion | flops 4718592 | bytes 2097153 | tf_op jit(solution)/shard_map/jit(_where)/select_n | solution.py:152
  106.8 1.8 %gather_fusion.1 = bf16[16,640]{1,0:T(8,128)(2,1)S(1)} fusion(bf16[512,640]{1,0:T(8,128)(2,1)} %constant_dynamic-update-slice_fusion.20, s32[1024]{0:T(1024)S(1)} %pad_clamp_fusion), kind=kCustom, calls=%fused_computation.1 | custom fusion | bytes 41024 | tf_op jit(solution)/shard_map/jit(_take)/gather | solution.py:135
  109.3 2.9 %fusion.18 = f32[256,256]{0,1:T(8,128)S(1)} fusion(bf16[256,5120]{1,0:T(8,128)(2,1)} %all-gather.2.cloned.1.call-done, bf16[640,8,2,128]{3,2,1,0:T(2,128)(2,1)S(1)} %bitcast.86, f32[256]{0:T(256)S(1)} %bitcast.96), kind=kOutput, calls=%fused_computation.29 | convolution fusion | flops 671154176 | bytes 5506048 | tf_op jit(solution)/shard_map/dot_general | solution.py:91
  113.3 3.7 %collective-permute-start.15 = (bf16[2,256,128]{2,1,0:T(8,128)(2,1)S(1)}, bf16[2,256,128]{2,1,0:T(8,128)(2,1)S(1)}, u32[]{:S(2)}, u32[]{:S(2)}) collective-permute-start(bf16[2,256,128]{2,1,0:T(8,128)(2,1)S(1)} %pad_maximum_fusion.1), channel_id=1, source_target_pairs={{0,1},{1,0},{2,3},{3,2},{4,5},{5,4},{6,7},{7,6},{8,9},{9,8},{10,11... | collective-permute-start | bytes 393224 | tf_op jit(solution)/shard_map/ppermute | solution.py:11
  117.0 5.9 %convolution_add_fusion = f32[256,640]{1,0:T(8,128)S(1)} fusion(bf16[256,5120]{1,0:T(8,128)(2,1)} %all-gather.2.cloned.1.call-done, bf16[5120,640]{1,0:T(8,128)(2,1)} %param.13, f32[640]{0:T(1024)S(1)} %copy-done.9), kind=kOutput, calls=%fused_computation.28 | convolution fusion | flops 1677885440 | bytes 9832960 | tf_op jit(solution)/shard_map/dot_general | solution.py:90
  124.2 7.2 %fusion.1 = (f32[256,5]{0,1:T(8,128)S(1)}, f32[256,5,2560]{2,0,1:T(8,128)}) fusion(pred[256,2560]{1,0:T(8,128)(4,1)S(1)} %compare_and_fusion, bf16[2,2048,128]{2,1,0:T(8,128)(2,1)} %maximum_select_fusion, bf16[2,512,128]{2,1,0:T(8,128)(2,1)S(1)} %maximum_select_fusion.1, bf16[256,5,64]{2,0,1:T(8,128)(2,1)S(1)} %get-tuple-element.25, ...), kind=kOutput, calls=%fused_computation.7 | convolution fusion | flops 850656000 | bytes 15406080 | tf_op jit(solution)/shard_map/ngd,md->ngm/dot_general | solution.py:32
  131.4 8.5 %fusion.2 = f32[256,5]{0,1:T(8,128)S(1)} fusion(f32[256,5,2560]{2,0,1:T(8,128)} %get-tuple-element.72, f32[256,5]{0,1:T(8,128)S(1)} %get-tuple-element.71, pred[256,2560]{1,0:T(8,128)(4,1)S(1)} %compare_and_fusion), kind=kLoop, calls=%fused_computation.8 | loop fusion | flops 13105920 | bytes 13772800 | tf_op jit(solution)/shard_map/reduce_sum | solution.py:39
  139.9 7.0 %fusion.40 = bf16[256,5,128]{0,2,1:T(8,128)(2,1)S(1)} fusion(f32[256,5,2560]{2,0,1:T(8,128)} %get-tuple-element.72, f32[256,5]{0,1:T(8,128)S(1)} %get-tuple-element.71, pred[256,2560]{1,0:T(8,128)(4,1)S(1)} %compare_and_fusion, bf16[2,512,128]{2,1,0:T(8,128)(2,1)S(1)} %maximum_select_fusion.1, bf16[2,2048,128]{2,1,0:T(8,128)(2,1)S(1)} %copy-done.1, ...), kind=kOutput, calls=%fused_computation.39 | convolution fusion | flops 853606400 | bytes 15411200 | tf_op jit(solution)/shard_map/ngm,md->ngd/dot_general | solution.py:41
  (134 shorter events, 34.9 us)
Async XLA Ops:
  7.2 8.3 %copy-start.16 = (s32[16]{0:T(128)S(1)}, s32[16]{0:T(128)}, u32[]{:S(2)}) copy-start(s32[16]{0:T(128)} %param.18) | copy-start | bytes 196
  7.2 9.1 %copy-start.5 = (bf16[16,1280]{1,0:T(8,128)(2,1)S(1)}, bf16[16,1280]{1,0:T(8,128)(2,1)}, u32[]{:S(2)}) copy-start(bf16[16,1280]{1,0:T(8,128)(2,1)} %param.11) | copy-start | bytes 122884
  7.2 18.9 %copy-start.12 = (f32[2,128]{1,0:T(2,128)S(1)}, f32[2,128]{1,0:T(2,128)}, u32[]{:S(2)}) copy-start(f32[2,128]{1,0:T(2,128)} %param.16) | copy-start | bytes 3076
  7.2 18.9 %copy-start = (bf16[5120,2,128]{2,1,0:T(2,128)(2,1)S(1)}, bf16[5120,2,128]{2,1,0:T(2,128)(2,1)}, u32[]{:S(2)}) copy-start(bf16[5120,2,128]{2,1,0:T(2,128)(2,1)} %param.14) | copy-start | bytes 7864324
  7.2 19.4 %copy-start.8 = (f32[640]{0:T(1024)S(1)}, f32[640]{0:T(1024)}, u32[]{:S(2)}) copy-start(f32[640]{0:T(1024)} %param.15) | copy-start | bytes 7684
  7.2 102.1 %all-gather.2.cloned.1.call-start = ((), (), s32[]{:S(2)}) async-start(), calls=%async_computation | async-start | bytes 3276800 | tf_op jit(solution)/shard_map/all_gather | solution.py:89
  14.0 86.8 %collective-permute-start.14 = (bf16[2,1024,128]{2,1,0:T(8,128)(2,1)}, bf16[2,1024,128]{2,1,0:T(8,128)(2,1)}, u32[]{:S(2)}, u32[]{:S(2)}) collective-permute-start(bf16[2,1024,128]{2,1,0:T(8,128)(2,1)} %param.20), channel_id=1, source_target_pairs={{0,1},{1,0},{2,3},{3,2},{4,5},{5,4},{6,7},{7,6},{8,9},{9,8},{10,11... | collective-permute-start | bytes 1572872 | tf_op jit(solution)/shard_map/ppermute | solution.py:11
  26.6 6.7 %copy-start.17 = (s32[16]{0:T(128)S(1)}, s32[16]{0:T(128)}, u32[]{:S(2)}) copy-start(s32[16]{0:T(128)} %param.21) | copy-start | bytes 196
  26.6 9.9 %copy-start.14 = (s32[16]{0:T(128)S(1)}, s32[16]{0:T(128)}, u32[]{:S(2)}) copy-start(s32[16]{0:T(128)} %param.19) | copy-start | bytes 196
  30.9 10.2 %collective-permute-start = (bf16[16,1024]{1,0:T(8,128)(2,1)S(1)}, bf16[16,1024]{1,0:T(8,128)(2,1)S(1)}, u32[]{:S(2)}, u32[]{:S(2)}) collective-permute-start(bf16[16,1024]{1,0:T(8,128)(2,1)S(1)} %concatenate.83), channel_id=1, source_target_pairs={{0,1},{1,0},{2,3},{3,2},{4,5},{5,4},{6,7},{7,6},{8,9},{9,8},{10,11... | collective-permute-start | bytes 98312 | tf_op jit(solution)/shard_map/ppermute | solution.py:76
  33.3 5.8 %copy-start.6 = (f32[64]{0:T(128)}, f32[64]{0:T(128)S(1)}, u32[]{:S(2)}) copy-start(f32[64]{0:T(128)S(1)} %negate_power_fusion) | copy-start | bytes 772
  41.2 5.7 %collective-permute-start.1 = (bf16[32,1024]{1,0:T(8,128)(2,1)S(1)}, bf16[32,1024]{1,0:T(8,128)(2,1)S(1)}, u32[]{:S(2)}, u32[]{:S(2)}) collective-permute-start(bf16[32,1024]{1,0:T(8,128)(2,1)S(1)} %pad_maximum_fusion.2), channel_id=1, source_target_pairs={{0,2},{1,3},{2,4},{3,5},{4,6},{5,7},{6,0},{7,1},{8,10},{9,11},{10,... | collective-permute-start | bytes 196616 | tf_op jit(solution)/shard_map/ppermute | solution.py:76
  42.5 6.2 %collective-permute-start.2 = (bf16[32,1024]{1,0:T(8,128)(2,1)S(1)}, bf16[32,1024]{1,0:T(8,128)(2,1)S(1)}, u32[]{:S(2)}, u32[]{:S(2)}) collective-permute-start(bf16[32,1024]{1,0:T(8,128)(2,1)S(1)} %pad_maximum_fusion.2), channel_id=1, source_target_pairs={{0,4},{1,5},{2,6},{3,7},{4,0},{5,1},{6,2},{7,3},{8,12},{9,13},{10,... | collective-permute-start | bytes 196616 | tf_op jit(solution)/shard_map/ppermute | solution.py:76
  45.1 4.2 %collective-permute-start.3 = (bf16[32,1024]{1,0:T(8,128)(2,1)S(1)}, bf16[32,1024]{1,0:T(8,128)(2,1)S(1)}, u32[]{:S(2)}, u32[]{:S(2)}) collective-permute-start(bf16[32,1024]{1,0:T(8,128)(2,1)S(1)} %pad_maximum_fusion.2), channel_id=1, source_target_pairs={{0,6},{1,7},{2,0},{3,1},{4,2},{5,3},{6,4},{7,5},{8,14},{9,15},{10,... | collective-permute-start | bytes 196616 | tf_op jit(solution)/shard_map/ppermute | solution.py:76
  50.0 9.9 %collective-permute-start.4 = (bf16[128,1024]{1,0:T(8,128)(2,1)}, bf16[128,1024]{1,0:T(8,128)(2,1)}, u32[]{:S(2)}, u32[]{:S(2)}) collective-permute-start(bf16[128,1024]{1,0:T(8,128)(2,1)} %get-tuple-element.36), channel_id=1, source_target_pairs={{0,8},{1,9},{2,10},{3,11},{4,12},{5,13},{6,14},{7,15},{8,16},{9,17... | collective-permute-start | bytes 786440 | tf_op jit(solution)/shard_map/ppermute | solution.py:76
  52.4 14.0 %collective-permute-start.5 = (bf16[128,1024]{1,0:T(8,128)(2,1)}, bf16[128,1024]{1,0:T(8,128)(2,1)}, u32[]{:S(2)}, u32[]{:S(2)}) collective-permute-start(bf16[128,1024]{1,0:T(8,128)(2,1)} %get-tuple-element.36), channel_id=1, source_target_pairs={{0,16},{1,17},{2,18},{3,19},{4,20},{5,21},{6,22},{7,23},{8,24},{9,... | collective-permute-start | bytes 786440 | tf_op jit(solution)/shard_map/ppermute | solution.py:76
  56.5 11.6 %collective-permute-start.6 = (bf16[128,1024]{1,0:T(8,128)(2,1)}, bf16[128,1024]{1,0:T(8,128)(2,1)}, u32[]{:S(2)}, u32[]{:S(2)}) collective-permute-start(bf16[128,1024]{1,0:T(8,128)(2,1)} %get-tuple-element.36), channel_id=1, source_target_pairs={{0,24},{1,25},{2,26},{3,27},{4,28},{5,29},{6,30},{7,31},{8,0},{9,1... | collective-permute-start | bytes 786440 | tf_op jit(solution)/shard_map/ppermute | solution.py:76
  79.2 5.4 %slice-start = ((s8[6291456]{0:T(1024)(128)(4,1)}), s8[4194304]{0:T(1024)(128)(4,1)S(1)}, s32[]{:S(2)}) async-start(s8[6291456]{0:T(1024)(128)(4,1)} %bitcast.83), calls=%async_computation.1 | async-start | bytes 8388608
  85.5 23.8 %copy-start.13 = (f32[2,128]{1,0:T(2,128)S(1)}, f32[2,128]{1,0:T(2,128)}, u32[]{:S(2)}) copy-start(f32[2,128]{1,0:T(2,128)} %param.16) | copy-start | bytes 3076
  85.5 4.3 %collective-permute-start.7 = (bf16[16,640]{1,0:T(8,128)(2,1)S(1)}, bf16[16,640]{1,0:T(8,128)(2,1)S(1)}, u32[]{:S(2)}, u32[]{:S(2)}) collective-permute-start(bf16[16,640]{1,0:T(8,128)(2,1)S(1)} %bitcast.93), channel_id=1, source_target_pairs={{0,1},{1,0},{2,3},{3,2},{4,5},{5,4},{6,7},{7,6},{8,9},{9,8},{10,11... | collective-permute-start | bytes 61448 | tf_op jit(solution)/shard_map/ppermute | solution.py:76
  90.4 4.1 %collective-permute-start.8 = (bf16[32,640]{1,0:T(8,128)(2,1)S(1)}, bf16[32,640]{1,0:T(8,128)(2,1)S(1)}, u32[]{:S(2)}, u32[]{:S(2)}) collective-permute-start(bf16[32,640]{1,0:T(8,128)(2,1)S(1)} %get-tuple-element.54), channel_id=1, source_target_pairs={{0,2},{1,3},{2,4},{3,5},{4,6},{5,7},{6,0},{7,1},{8,10},{9,11},{10,... | collective-permute-start | bytes 122888 | tf_op jit(solution)/shard_map/ppermute | solution.py:76
  90.6 4.8 %collective-permute-start.9 = (bf16[32,640]{1,0:T(8,128)(2,1)S(1)}, bf16[32,640]{1,0:T(8,128)(2,1)S(1)}, u32[]{:S(2)}, u32[]{:S(2)}) collective-permute-start(bf16[32,640]{1,0:T(8,128)(2,1)S(1)} %get-tuple-element.54), channel_id=1, source_target_pairs={{0,4},{1,5},{2,6},{3,7},{4,0},{5,1},{6,2},{7,3},{8,12},{9,13},{10,... | collective-permute-start | bytes 122888 | tf_op jit(solution)/shard_map/ppermute | solution.py:76
  93.2 3.1 %collective-permute-start.10 = (bf16[32,640]{1,0:T(8,128)(2,1)S(1)}, bf16[32,640]{1,0:T(8,128)(2,1)S(1)}, u32[]{:S(2)}, u32[]{:S(2)}) collective-permute-start(bf16[32,640]{1,0:T(8,128)(2,1)S(1)} %get-tuple-element.54), channel_id=1, source_target_pairs={{0,6},{1,7},{2,0},{3,1},{4,2},{5,3},{6,4},{7,5},{8,14},{9,15},{10,... | collective-permute-start | bytes 122888 | tf_op jit(solution)/shard_map/ppermute | solution.py:76
  96.9 6.8 %collective-permute-start.11 = (bf16[128,640]{1,0:T(8,128)(2,1)S(1)}, bf16[128,640]{1,0:T(8,128)(2,1)S(1)}, u32[]{:S(2)}, u32[]{:S(2)}) collective-permute-start(bf16[128,640]{1,0:T(8,128)(2,1)S(1)} %get-tuple-element.42), channel_id=1, source_target_pairs={{0,8},{1,9},{2,10},{3,11},{4,12},{5,13},{6,14},{7,15},{8,16},{9,17... | collective-permute-start | bytes 491528 | tf_op jit(solution)/shard_map/ppermute | solution.py:76
  97.4 7.7 %collective-permute-start.12 = (bf16[128,640]{1,0:T(8,128)(2,1)S(1)}, bf16[128,640]{1,0:T(8,128)(2,1)S(1)}, u32[]{:S(2)}, u32[]{:S(2)}) collective-permute-start(bf16[128,640]{1,0:T(8,128)(2,1)S(1)} %get-tuple-element.42), channel_id=1, source_target_pairs={{0,16},{1,17},{2,18},{3,19},{4,20},{5,21},{6,22},{7,23},{8,24},{9,... | collective-permute-start | bytes 491528 | tf_op jit(solution)/shard_map/ppermute | solution.py:76
  99.1 7.1 %collective-permute-start.13 = (bf16[128,640]{1,0:T(8,128)(2,1)S(1)}, bf16[128,640]{1,0:T(8,128)(2,1)S(1)}, u32[]{:S(2)}, u32[]{:S(2)}) collective-permute-start(bf16[128,640]{1,0:T(8,128)(2,1)S(1)} %get-tuple-element.42), channel_id=1, source_target_pairs={{0,24},{1,25},{2,26},{3,27},{4,28},{5,29},{6,30},{7,31},{8,0},{9,1... | collective-permute-start | bytes 491528 | tf_op jit(solution)/shard_map/ppermute | solution.py:76
  105.8 6.8 %copy-start.7 = (f32[64]{0:T(128)S(1)}, f32[64]{0:T(128)}, u32[]{:S(2)}) copy-start(f32[64]{0:T(128)} %copy-done.6) | copy-start | bytes 772
  105.8 6.8 %copy-start.11 = (f32[256]{0:T(256)S(1)}, f32[256]{0:T(256)}, u32[]{:S(2)}) copy-start(f32[256]{0:T(256)} %copy-done.10) | copy-start | bytes 3076
  109.3 7.7 %copy-start.9 = (f32[640]{0:T(1024)S(1)}, f32[640]{0:T(1024)}, u32[]{:S(2)}) copy-start(f32[640]{0:T(1024)} %param.15) | copy-start | bytes 7684
  113.3 9.6 %copy-start.4 = (bf16[2,256,128]{2,1,0:T(8,128)(2,1)}, bf16[2,256,128]{2,1,0:T(8,128)(2,1)S(1)}, u32[]{:S(2)}) copy-start(bf16[2,256,128]{2,1,0:T(8,128)(2,1)S(1)} %pad_maximum_fusion.1) | copy-start | bytes 393220
  113.3 10.7 %collective-permute-start.15 = (bf16[2,256,128]{2,1,0:T(8,128)(2,1)S(1)}, bf16[2,256,128]{2,1,0:T(8,128)(2,1)S(1)}, u32[]{:S(2)}, u32[]{:S(2)}) collective-permute-start(bf16[2,256,128]{2,1,0:T(8,128)(2,1)S(1)} %pad_maximum_fusion.1), channel_id=1, source_target_pairs={{0,1},{1,0},{2,3},{3,2},{4,5},{5,4},{6,7},{7,6},{8,9},{9,8},{10,11... | collective-permute-start | bytes 393224 | tf_op jit(solution)/shard_map/ppermute | solution.py:11
  131.4 8.5 %copy-start.1 = (bf16[2,2048,128]{2,1,0:T(8,128)(2,1)S(1)}, bf16[2,2048,128]{2,1,0:T(8,128)(2,1)}, u32[]{:S(2)}) copy-start(bf16[2,2048,128]{2,1,0:T(8,128)(2,1)} %maximum_select_fusion) | copy-start | bytes 3145732
  (5 other events, 14.6 us)
Sparse Core Ops, SparseCore 0:
  14.1 38.1 all-gather.1
where the time goes:
time: 155 us
  local copies, waits for them, and re-layouts  32.2 us (21%)
  matrix products  32 us (21%)
  starting transfers between devices  27.6 us (18%)
  other arithmetic  27.3 us (18%)
  between operations  15.1 us (10%)
  waiting for transfers between devices  10.5 us (7%)
  blocking collectives  9.84 us (6%)
    ppermute x14, starting transfers between devices, tree_gather(): parts.append(lax.ppermute(buffer, 'tok', pairs))  22.4 us
    unnamed x60, local copies, waits for them, and re-layouts  18.3 us
    dot_general x2, matrix products, head_scores(): jnp.einsum('ngd,md->ngm', shaped, key_rows, preferred_element_type=jnp.fl...  10.7 us
    ppermute x14, waiting for transfers between devices, tree_gather(): parts.append(lax.ppermute(buffer, 'tok', pairs))  10.5 us
    dot_general x2, matrix products, project(): query = jnp.dot(cols, w_query, preferred_element_type=jnp.float32) + b_query  10.1 us
    all_gather x1, blocking collectives, project(): cols = lax.all_gather(rows, 'kv', axis=1, tiled=True)  9.84 us
    reduce_sum x2, other arithmetic, head_mix(): totals = jnp.sum(powers, axis=-1)  9.29 us
    dot_general x2, matrix products, head_mix(): jnp.einsum('ngm,md->ngd', weights, value_rows, preferred_element_type=jnp...  7.83 us
  transfers between devices with their start and end apart: 17, of which 9 were waited for; matrix products, arithmetic and copies ran while one was open for 37% of the time, Pallas kernels for 0%

commit v1 on v0

--- a/solution.py
+++ b/solution.py
@@ -5,6 +5,11 @@
 
 HD = 128
 THETA = 1000000.0
+
+
+def gather_by_exchange(x, axis, dim):
+    copies = jnp.concatenate([x] * lax.axis_size(axis), axis=dim)
+    return lax.all_to_all(copies, axis, dim, dim, tiled=True)
 
 
 def swapped(value, axis, distance):
@@ -86,7 +91,7 @@
 
 
 def project(rows, w_query, kv_weight, b_query, kv_bias):
-    cols = lax.all_gather(rows, "kv", axis=1, tiled=True)
+    cols = gather_by_exchange(rows, "kv", 1)
     query = jnp.dot(cols, w_query, preferred_element_type=jnp.float32) + b_query
     keyval = jnp.dot(cols, kv_weight, preferred_element_type=jnp.float32) + kv_bias
     return (query, keyval)

time: 155 us -> 129 us (0.83)
  between operations: 15.1 us -> 1.85 us
  local copies, waits for them, and re-layouts: 32.2 us -> 22.1 us
  blocking collectives: 9.84 us -> 0 us
  waiting for transfers between devices: 10.5 us -> 19.1 us
  starting transfers between devices: 27.6 us -> 35.5 us
  other arithmetic: 27.3 us -> 21 us
  matrix products: 32 us -> 28.8 us
    all_gather x1 -> x0, blocking collectives: 9.84 us -> none  [project(): cols = lax.all_gather(rows, 'kv', axis=1, tiled=True)]
    unnamed x60 -> x55, local copies, waits for them, and re-layouts: 18.3 us -> 9.27 us
    all_to_all x0 -> x2, starting transfers between devices: none -> 8.8 us  [gather_by_exchange(): return lax.all_to_all(copies, axis, dim, dim, tiled=True)]
    ppermute x14, waiting for transfers between devices: 10.5 us -> 18.9 us  [tree_gather(): parts.append(lax.ppermute(buffer, 'tok', pairs))]
    all_to_all x0 -> x4, local copies, waits for them, and re-layouts: none -> 7.84 us  [gather_by_exchange(): return lax.all_to_all(copies, axis, dim, dim, tiled=True)]
    dot_general x2, matrix products: 10.1 us -> 6.1 us  [project(): query = jnp.dot(cols, w_query, preferred_element_type=jnp.float32) + b_query]
    concatenate x4, local copies, waits for them, and re-layouts: 3.6 us -> 0.06 us  [tree_gather(): buffer = jnp.concatenate(parts, axis=0)]
  transfers between devices with their start and end apart: 17 -> 18, of which waited for: 9 -> 12; matrix products, arithmetic and copies ran while one was open for 37% -> 22% of each run, Pallas kernels for 0% -> 0%
where the time goes in v1:
time: 129 us; the launch traced here: 128 us
  starting transfers between devices  35.5 us (28%)
  matrix products  28.8 us (22%)
  local copies, waits for them, and re-layouts  22.1 us (17%)
  other arithmetic  21 us (16%)
  waiting for transfers between devices  19.1 us (15%)
  between operations  1.85 us (1%)
    ppermute x14, starting transfers between devices, tree_gather(): parts.append(lax.ppermute(buffer, 'tok', pairs))  21.9 us
    ppermute x14, waiting for transfers between devices, tree_gather(): parts.append(lax.ppermute(buffer, 'tok', pairs))  18.9 us
    dot_general x2, matrix products, head_scores(): jnp.einsum('ngd,md->ngm', shaped, key_rows, preferred_element_type=jnp.fl...  10.6 us
    reduce_sum x2, other arithmetic, head_mix(): totals = jnp.sum(powers, axis=-1)  9.29 us
    unnamed x55, local copies, waits for them, and re-layouts  9.27 us
    all_to_all x2, starting transfers between devices, gather_by_exchange(): return lax.all_to_all(copies, axis, dim, dim, tiled=True)  8.8 us
    all_to_all x4, local copies, waits for them, and re-layouts, gather_by_exchange(): return lax.all_to_all(copies, axis, dim, dim, tiled=True)  7.84 us
    dot_general x2, matrix products, head_mix(): jnp.einsum('ngm,md->ngd', weights, value_rows, preferred_element_type=jnp...  7.83 us
  transfers between devices with their start and end apart: 18, of which 12 were waited for; matrix products, arithmetic and copies ran while one was open for 22% of the time, Pallas kernels for 0%

profile of v1, /device:TPU:1, one launch (start us, length us, event | category | flops | bytes accessed | tf_op | source)
XLA Modules:
  0.0 128.3 jit_solution(14175342797987073880)
XLA Ops:
  0.7 6.5 %copy.178 = bf16[2,12288,128]{2,1,0:T(8,128)(2,1)} copy(bf16[2,12288,128]{2,1,0:T(8,128)(2,1)} %param.17) | data formatting | bytes 12582912
  7.2 1.4 %collective-permute-start.14 = (bf16[2,1024,128]{2,1,0:T(8,128)(2,1)}, bf16[2,1024,128]{2,1,0:T(8,128)(2,1)}, u32[]{:S(2)}, u32[]{:S(2)}) collective-permute-start(bf16[2,1024,128]{2,1,0:T(8,128)(2,1)} %param.20), channel_id=1, source_target_pairs={{0,1},{1,0},{2,3},{3,2},{4,5},{5,4},{6,7},{7,6},{8,9},{9,8},{10,11... | collective-permute-start | bytes 1572872 | tf_op jit(solution)/shard_map/ppermute | solution.py:16
  9.2 4.1 %all-to-all-start = ((bf16[16,4,1280]{2,0,1:T(8,128)(2,1)}), bf16[16,4,1280]{2,0,1:T(8,128)(2,1)S(1)}, u32[]{:S(2)}, u32[]{:S(2)}) async-start(bf16[16,4,1280]{2,0,1:T(8,128)(2,1)} %bitcast.88), calls=%async_computation | async-start | bytes 327680 | tf_op jit(solution)/shard_map/all_to_all | solution.py:12
  16.8 2.6 %copy.97 = bf16[256,4,1280]{2,0,1:T(8,128)(2,1)} copy(bf16[256,4,1280]{0,2,1:T(8,128)(2,1)S(1)} %bitcast.97) | data formatting | bytes 5242880 | tf_op jit(solution)/shard_map/all_to_all | solution.py:12
  20.2 1.3 %compare_and_fusion = pred[256,2560]{1,0:T(8,128)(4,1)} fusion(s32[2560]{0:T(1024)S(1)} %add_select_fusion, s32[256]{0:T(256)S(1)} %iota_add_fusion, pred[2560]{0:T(1024)(128)(4,1)S(1)} %fusion.68), kind=kLoop, calls=%fused_computation.23 | loop fusion | flops 1310720 | bytes 669184 | tf_op jit(solution)/shard_map/and | solution.py:171
  21.5 1.2 multiply_cosine_fusion.1
  22.7 4.7 %all-to-all-start.1 = ((bf16[256,4,1280]{2,0,1:T(8,128)(2,1)}), bf16[256,4,1280]{2,0,1:T(8,128)(2,1)}, u32[]{:S(2)}, u32[]{:S(2)}) async-start(bf16[256,4,1280]{2,0,1:T(8,128)(2,1)} %copy.97), calls=%async_computation.1 | async-start | bytes 5242880 | tf_op jit(solution)/shard_map/all_to_all | solution.py:12
  27.9 3.8 %fusion.21 = bf16[16,640]{1,0:T(8,128)(2,1)S(1)} fusion(bf16[16,5120]{1,0:T(8,128)(2,1)S(1)} %bitcast.102, bf16[5120,640]{1,0:T(8,128)(2,1)} %param.13, f32[640]{0:T(1024)S(1)} %copy-done.8), kind=kOutput, calls=%fused_computation.32 | convolution fusion | flops 104878080 | bytes 6740480 | tf_op jit(solution)/shard_map/dot_general | solution.py:95
  33.2 1.3 %collective-permute-start.1 = (bf16[32,1024]{1,0:T(8,128)(2,1)S(1)}, bf16[32,1024]{1,0:T(8,128)(2,1)S(1)}, u32[]{:S(2)}, u32[]{:S(2)}) collective-permute-start(bf16[32,1024]{1,0:T(8,128)(2,1)S(1)} %pad_maximum_fusion.4), channel_id=1, source_target_pairs={{0,2},{1,3},{2,4},{3,5},{4,6},{5,7},{6,0},{7,1},{8,10},{9,11},{10,... | collective-permute-start | bytes 196616 | tf_op jit(solution)/shard_map/ppermute | solution.py:81
  34.5 2.6 %collective-permute-start.2 = (bf16[32,1024]{1,0:T(8,128)(2,1)S(1)}, bf16[32,1024]{1,0:T(8,128)(2,1)S(1)}, u32[]{:S(2)}, u32[]{:S(2)}) collective-permute-start(bf16[32,1024]{1,0:T(8,128)(2,1)S(1)} %pad_maximum_fusion.4), channel_id=1, source_target_pairs={{0,4},{1,5},{2,6},{3,7},{4,0},{5,1},{6,2},{7,3},{8,12},{9,13},{10,... | collective-permute-start | bytes 196616 | tf_op jit(solution)/shard_map/ppermute | solution.py:81
  38.2 1.8 %collective-permute-done.2 = bf16[32,1024]{1,0:T(8,128)(2,1)S(1)} collective-permute-done((bf16[32,1024]{1,0:T(8,128)(2,1)S(1)}, bf16[32,1024]{1,0:T(8,128)(2,1)S(1)}, u32[]{:S(2)}, u32[]{:S(2)}) %collective-permute-start.2) | collective-permute-done | bytes 65568 | tf_op jit(solution)/shard_map/ppermute | solution.py:81
  40.6 1.7 %collective-permute-start.4 = (bf16[128,1024]{1,0:T(8,128)(2,1)S(1)}, bf16[128,1024]{1,0:T(8,128)(2,1)S(1)}, u32[]{:S(2)}, u32[]{:S(2)}) collective-permute-start(bf16[128,1024]{1,0:T(8,128)(2,1)S(1)} %get-tuple-element.44), channel_id=1, source_target_pairs={{0,8},{1,9},{2,10},{3,11},{4,12},{5,13},{6,14},{7,15},{8,16},{9,17... | collective-permute-start | bytes 786440 | tf_op jit(solution)/shard_map/ppermute | solution.py:81
  42.4 3.4 %collective-permute-start.5 = (bf16[128,1024]{1,0:T(8,128)(2,1)S(1)}, bf16[128,1024]{1,0:T(8,128)(2,1)S(1)}, u32[]{:S(2)}, u32[]{:S(2)}) collective-permute-start(bf16[128,1024]{1,0:T(8,128)(2,1)S(1)} %get-tuple-element.44), channel_id=1, source_target_pairs={{0,16},{1,17},{2,18},{3,19},{4,20},{5,21},{6,22},{7,23},{8,24},{9,... | collective-permute-start | bytes 786440 | tf_op jit(solution)/shard_map/ppermute | solution.py:81
  46.6 3.0 %collective-permute-done.4 = bf16[128,1024]{1,0:T(8,128)(2,1)S(1)} collective-permute-done((bf16[128,1024]{1,0:T(8,128)(2,1)S(1)}, bf16[128,1024]{1,0:T(8,128)(2,1)S(1)}, u32[]{:S(2)}, u32[]{:S(2)}) %collective-permute-start.4) | collective-permute-done | bytes 262176 | tf_op jit(solution)/shard_map/ppermute | solution.py:81
  49.6 6.5 %collective-permute-done.5 = bf16[128,1024]{1,0:T(8,128)(2,1)S(1)} collective-permute-done((bf16[128,1024]{1,0:T(8,128)(2,1)S(1)}, bf16[128,1024]{1,0:T(8,128)(2,1)S(1)}, u32[]{:S(2)}, u32[]{:S(2)}) %collective-permute-start.5) | collective-permute-done | bytes 262176 | tf_op jit(solution)/shard_map/ppermute | solution.py:81
  57.4 2.3 %scatter_fusion = bf16[2,12288,128]{2,1,0:T(8,128)(2,1)} fusion(bf16[2,12288,128]{2,1,0:T(8,128)(2,1)} %copy.178, s32[16]{0:T(128)S(1)} %get-tuple-element.30, bf16[16,2,128]{2,0,1:T(8,128)(2,1)S(1)} %maximum_bitcast_fusion), kind=kCustom, calls=%fused_computation.2 | custom fusion | bytes 24640 | tf_op jit(solution)/shard_map/scatter | solution.py:61
  59.8 3.4 %fusion.100 = (f32[16,5]{0,1:T(8,128)S(1)}, f32[16,5,12288]{2,0,1:T(8,128)S(1)}) fusion(bf16[2,12288,128]{2,1,0:T(8,128)(2,1)} %scatter_fusion, bf16[16,5,64]{2,0,1:T(8,128)(2,1)S(1)} %get-tuple-element.41, bf16[16,5,64]{2,0,1:T(8,128)(2,1)S(1)} %get-tuple-element.40, pred[16,12288]{1,0:T(8,128)(4,1)S(1)} %fusion.43), kind=kOutput, calls=%fused_computation.195 | convolution fusion | flops 254648240 | bytes 7295296 | tf_op jit(solution)/shard_map/ngd,md->ngm/dot_general | solution.py:37
  64.8 2.3 %collective-permute-start.7 = (bf16[16,640]{1,0:T(8,128)(2,1)S(1)}, bf16[16,640]{1,0:T(8,128)(2,1)S(1)}, u32[]{:S(2)}, u32[]{:S(2)}) collective-permute-start(bf16[16,640]{1,0:T(8,128)(2,1)S(1)} %bitcast.110), channel_id=1, source_target_pairs={{0,1},{1,0},{2,3},{3,2},{4,5},{5,4},{6,7},{7,6},{8,9},{9,8},{10,11... | collective-permute-start | bytes 61448 | tf_op jit(solution)/shard_map/ppermute | solution.py:81
  68.4 3.3 %collective-permute-start.9 = (bf16[32,640]{1,0:T(8,128)(2,1)S(1)}, bf16[32,640]{1,0:T(8,128)(2,1)S(1)}, u32[]{:S(2)}, u32[]{:S(2)}) collective-permute-start(bf16[32,640]{1,0:T(8,128)(2,1)S(1)} %get-tuple-element.62), channel_id=1, source_target_pairs={{0,4},{1,5},{2,6},{3,7},{4,0},{5,1},{6,2},{7,3},{8,12},{9,13},{10,... | collective-permute-start | bytes 122888 | tf_op jit(solution)/shard_map/ppermute | solution.py:81
  72.3 1.4 %collective-permute-done.9 = bf16[32,640]{1,0:T(8,128)(2,1)S(1)} collective-permute-done((bf16[32,640]{1,0:T(8,128)(2,1)S(1)}, bf16[32,640]{1,0:T(8,128)(2,1)S(1)}, u32[]{:S(2)}, u32[]{:S(2)}) %collective-permute-start.9) | collective-permute-done | bytes 40992 | tf_op jit(solution)/shard_map/ppermute | solution.py:81
  74.7 1.1 collective-permute-start.11
  75.8 2.1 %collective-permute-start.12 = (bf16[128,640]{1,0:T(8,128)(2,1)S(1)}, bf16[128,640]{1,0:T(8,128)(2,1)S(1)}, u32[]{:S(2)}, u32[]{:S(2)}) collective-permute-start(bf16[128,640]{1,0:T(8,128)(2,1)S(1)} %get-tuple-element.50), channel_id=1, source_target_pairs={{0,16},{1,17},{2,18},{3,19},{4,20},{5,21},{6,22},{7,23},{8,24},{9,... | collective-permute-start | bytes 491528 | tf_op jit(solution)/shard_map/ppermute | solution.py:81
  77.9 2.8 %maximum_select_fusion = bf16[2,2048,128]{2,1,0:T(8,128)(2,1)} fusion(bf16[2,1024,128]{2,1,0:T(8,128)(2,1)} %collective-permute-done.14, bf16[2,1024,128]{2,1,0:T(8,128)(2,1)} %param.20, pred[]{:T(512)S(6)} %eq.32), kind=kLoop, calls=%fused_computation.38 | loop fusion | flops 4718592 | bytes 2097153 | tf_op jit(solution)/shard_map/jit(_where)/select_n | solution.py:157
  81.8 1.8 %collective-permute-done.12 = bf16[128,640]{1,0:T(8,128)(2,1)S(1)} collective-permute-done((bf16[128,640]{1,0:T(8,128)(2,1)S(1)}, bf16[128,640]{1,0:T(8,128)(2,1)S(1)}, u32[]{:S(2)}, u32[]{:S(2)}) %collective-permute-start.12) | collective-permute-done | bytes 163872 | tf_op jit(solution)/shard_map/ppermute | solution.py:81
  83.7 1.6 %collective-permute-done.13 = bf16[128,640]{1,0:T(8,128)(2,1)S(1)} collective-permute-done((bf16[128,640]{1,0:T(8,128)(2,1)S(1)}, bf16[128,640]{1,0:T(8,128)(2,1)S(1)}, u32[]{:S(2)}, u32[]{:S(2)}) %collective-permute-start.13) | collective-permute-done | bytes 163872 | tf_op jit(solution)/shard_map/ppermute | solution.py:81
  86.6 4.5 %copy.98 = bf16[256,4,1280]{0,2,1:T(8,128)(2,1)} copy(bf16[256,4,1280]{2,0,1:T(8,128)(2,1)} %all-to-all-done.1) | data formatting | bytes 5242880 | tf_op jit(solution)/shard_map/all_to_all | solution.py:12
  91.2 3.8 %fusion.18 = f32[256,256]{0,1:T(8,128)S(1)} fusion(bf16[256,5120]{0,1:T(8,128)(2,1)} %bitcast.95, bf16[640,8,2,128]{3,2,1,0:T(2,128)(2,1)} %bitcast.98, f32[256]{0:T(256)S(1)} %bitcast.113), kind=kOutput, calls=%fused_computation.30 | convolution fusion | flops 671154176 | bytes 5506048 | tf_op jit(solution)/shard_map/dot_general | solution.py:96
  95.7 2.3 %convolution_add_fusion = f32[256,640]{1,0:T(8,128)S(1)} fusion(bf16[256,5120]{0,1:T(8,128)(2,1)S(1)} %bitcast.96, bf16[5120,640]{1,0:T(8,128)(2,1)S(1)} %bitcast.92, f32[640]{0:T(1024)S(1)} %copy-done.8), kind=kOutput, calls=%fused_computation.29 | convolution fusion | flops 1677885440 | bytes 9832960 | tf_op jit(solution)/shard_map/dot_general | solution.py:95
  99.0 3.4 %collective-permute-start.15 = (bf16[2,256,128]{2,1,0:T(8,128)(2,1)S(1)}, bf16[2,256,128]{2,1,0:T(8,128)(2,1)}, u32[]{:S(2)}, u32[]{:S(2)}) collective-permute-start(bf16[2,256,128]{2,1,0:T(8,128)(2,1)S(1)} %pad_maximum_fusion.3), channel_id=1, source_target_pairs={{0,1},{1,0},{2,3},{3,2},{4,5},{5,4},{6,7},{7,6},{8,9},{9,8},{10,11... | collective-permute-start | bytes 393224 | tf_op jit(solution)/shard_map/ppermute | solution.py:16
  104.7 7.2 %fusion.1 = (f32[256,5]{0,1:T(8,128)S(1)}, f32[256,5,2560]{2,0,1:T(8,128)}) fusion(pred[256,2560]{1,0:T(8,128)(4,1)S(1)} %copy-done.2, bf16[2,2048,128]{2,1,0:T(8,128)(2,1)} %maximum_select_fusion, bf16[2,512,128]{2,1,0:T(8,128)(2,1)S(1)} %maximum_select_fusion.1, bf16[256,5,64]{2,0,1:T(8,128)(2,1)S(1)} %get-tuple-element.33, ...), kind=kOutput, calls=%fused_computation.7 | convolution fusion | flops 850656000 | bytes 15406080 | tf_op jit(solution)/shard_map/ngd,md->ngm/dot_general | solution.py:37
  111.9 8.5 %fusion.2 = f32[256,5]{0,1:T(8,128)S(1)} fusion(f32[256,5,2560]{2,0,1:T(8,128)} %get-tuple-element.80, f32[256,5]{0,1:T(8,128)S(1)} %get-tuple-element.79, pred[256,2560]{1,0:T(8,128)(4,1)S(1)} %copy-done.2), kind=kLoop, calls=%fused_computation.8 | loop fusion | flops 13105920 | bytes 13772800 | tf_op jit(solution)/shard_map/reduce_sum | solution.py:44
  120.4 7.0 %fusion.40 = bf16[256,5,128]{0,2,1:T(8,128)(2,1)S(1)} fusion(f32[256,5,2560]{2,0,1:T(8,128)} %get-tuple-element.80, f32[256,5]{0,1:T(8,128)S(1)} %get-tuple-element.79, pred[256,2560]{1,0:T(8,128)(4,1)S(1)} %copy-done.2, bf16[2,512,128]{2,1,0:T(8,128)(2,1)S(1)} %maximum_select_fusion.1, bf16[2,2048,128]{2,1,0:T(8,128)(2,1)S(1)} %copy-done.3, ...), kind=kOutput, calls=%fused_computation.40 | convolution fusion | flops 853606400 | bytes 15411200 | tf_op jit(solution)/shard_map/ngm,md->ngd/dot_general | solution.py:46
  (136 shorter events, 21.5 us)
Async XLA Ops:
  0.6 7.9 %copy-start.7 = (bf16[16,1280]{1,0:T(8,128)(2,1)S(1)}, bf16[16,1280]{1,0:T(8,128)(2,1)}, u32[]{:S(2)}) copy-start(bf16[16,1280]{1,0:T(8,128)(2,1)} %param.11) | copy-start | bytes 122884
  0.6 12.8 %copy-start.12 = (s32[16]{0:T(128)S(1)}, s32[16]{0:T(128)}, u32[]{:S(2)}) copy-start(s32[16]{0:T(128)} %param.21) | copy-start | bytes 196
  0.7 15.4 %copy-start.4 = (bf16[256,1280]{1,0:T(8,128)(2,1)S(1)}, bf16[256,1280]{1,0:T(8,128)(2,1)}, u32[]{:S(2)}) copy-start(bf16[256,1280]{1,0:T(8,128)(2,1)} %param.12) | copy-start | bytes 1966084
  7.2 70.8 %collective-permute-start.14 = (bf16[2,1024,128]{2,1,0:T(8,128)(2,1)}, bf16[2,1024,128]{2,1,0:T(8,128)(2,1)}, u32[]{:S(2)}, u32[]{:S(2)}) collective-permute-start(bf16[2,1024,128]{2,1,0:T(8,128)(2,1)} %param.20), channel_id=1, source_target_pairs={{0,1},{1,0},{2,3},{3,2},{4,5},{5,4},{6,7},{7,6},{8,9},{9,8},{10,11... | collective-permute-start | bytes 1572872 | tf_op jit(solution)/shard_map/ppermute | solution.py:16
  9.2 13.4 %all-to-all-start = ((bf16[16,4,1280]{2,0,1:T(8,128)(2,1)}), bf16[16,4,1280]{2,0,1:T(8,128)(2,1)S(1)}, u32[]{:S(2)}, u32[]{:S(2)}) async-start(bf16[16,4,1280]{2,0,1:T(8,128)(2,1)} %bitcast.88), calls=%async_computation | async-start | bytes 327680 | tf_op jit(solution)/shard_map/all_to_all | solution.py:12
  19.4 8.0 %copy-start.1 = (bf16[5120,2,128]{2,1,0:T(2,128)(2,1)S(1)}, bf16[5120,2,128]{2,1,0:T(2,128)(2,1)}, u32[]{:S(2)}) copy-start(bf16[5120,2,128]{2,1,0:T(2,128)(2,1)} %param.14) | copy-start | bytes 7864324
  19.4 8.0 %copy-start.9 = (f32[2,128]{1,0:T(2,128)S(1)}, f32[2,128]{1,0:T(2,128)}, u32[]{:S(2)}) copy-start(f32[2,128]{1,0:T(2,128)} %param.16) | copy-start | bytes 3076
  22.7 5.2 %copy-start.8 = (f32[640]{0:T(1024)S(1)}, f32[640]{0:T(1024)}, u32[]{:S(2)}) copy-start(f32[640]{0:T(1024)} %param.15) | copy-start | bytes 7684
  22.7 63.9 %all-to-all-start.1 = ((bf16[256,4,1280]{2,0,1:T(8,128)(2,1)}), bf16[256,4,1280]{2,0,1:T(8,128)(2,1)}, u32[]{:S(2)}, u32[]{:S(2)}) async-start(bf16[256,4,1280]{2,0,1:T(8,128)(2,1)} %copy.97), calls=%async_computation.1 | async-start | bytes 5242880 | tf_op jit(solution)/shard_map/all_to_all | solution.py:12
  31.8 1.4 %collective-permute-start = (bf16[16,1024]{1,0:T(8,128)(2,1)S(1)}, bf16[16,1024]{1,0:T(8,128)(2,1)S(1)}, u32[]{:S(2)}, u32[]{:S(2)}) collective-permute-start(bf16[16,1024]{1,0:T(8,128)(2,1)S(1)} %concatenate.90), channel_id=1, source_target_pairs={{0,1},{1,0},{2,3},{3,2},{4,5},{5,4},{6,7},{7,6},{8,9},{9,8},{10,11... | collective-permute-start | bytes 98312 | tf_op jit(solution)/shard_map/ppermute | solution.py:81
  33.2 5.0 %collective-permute-start.1 = (bf16[32,1024]{1,0:T(8,128)(2,1)S(1)}, bf16[32,1024]{1,0:T(8,128)(2,1)S(1)}, u32[]{:S(2)}, u32[]{:S(2)}) collective-permute-start(bf16[32,1024]{1,0:T(8,128)(2,1)S(1)} %pad_maximum_fusion.4), channel_id=1, source_target_pairs={{0,2},{1,3},{2,4},{3,5},{4,6},{5,7},{6,0},{7,1},{8,10},{9,11},{10,... | collective-permute-start | bytes 196616 | tf_op jit(solution)/shard_map/ppermute | solution.py:81
  34.5 5.6 %collective-permute-start.2 = (bf16[32,1024]{1,0:T(8,128)(2,1)S(1)}, bf16[32,1024]{1,0:T(8,128)(2,1)S(1)}, u32[]{:S(2)}, u32[]{:S(2)}) collective-permute-start(bf16[32,1024]{1,0:T(8,128)(2,1)S(1)} %pad_maximum_fusion.4), channel_id=1, source_target_pairs={{0,4},{1,5},{2,6},{3,7},{4,0},{5,1},{6,2},{7,3},{8,12},{9,13},{10,... | collective-permute-start | bytes 196616 | tf_op jit(solution)/shard_map/ppermute | solution.py:81
  37.1 3.5 %collective-permute-start.3 = (bf16[32,1024]{1,0:T(8,128)(2,1)S(1)}, bf16[32,1024]{1,0:T(8,128)(2,1)S(1)}, u32[]{:S(2)}, u32[]{:S(2)}) collective-permute-start(bf16[32,1024]{1,0:T(8,128)(2,1)S(1)} %pad_maximum_fusion.4), channel_id=1, source_target_pairs={{0,6},{1,7},{2,0},{3,1},{4,2},{5,3},{6,4},{7,5},{8,14},{9,15},{10,... | collective-permute-start | bytes 196616 | tf_op jit(solution)/shard_map/ppermute | solution.py:81
  40.6 9.0 %collective-permute-start.4 = (bf16[128,1024]{1,0:T(8,128)(2,1)S(1)}, bf16[128,1024]{1,0:T(8,128)(2,1)S(1)}, u32[]{:S(2)}, u32[]{:S(2)}) collective-permute-start(bf16[128,1024]{1,0:T(8,128)(2,1)S(1)} %get-tuple-element.44), channel_id=1, source_target_pairs={{0,8},{1,9},{2,10},{3,11},{4,12},{5,13},{6,14},{7,15},{8,16},{9,17... | collective-permute-start | bytes 786440 | tf_op jit(solution)/shard_map/ppermute | solution.py:81
  42.4 13.6 %collective-permute-start.5 = (bf16[128,1024]{1,0:T(8,128)(2,1)S(1)}, bf16[128,1024]{1,0:T(8,128)(2,1)S(1)}, u32[]{:S(2)}, u32[]{:S(2)}) collective-permute-start(bf16[128,1024]{1,0:T(8,128)(2,1)S(1)} %get-tuple-element.44), channel_id=1, source_target_pairs={{0,16},{1,17},{2,18},{3,19},{4,20},{5,21},{6,22},{7,23},{8,24},{9,... | collective-permute-start | bytes 786440 | tf_op jit(solution)/shard_map/ppermute | solution.py:81
  45.8 10.4 %collective-permute-start.6 = (bf16[128,1024]{1,0:T(8,128)(2,1)S(1)}, bf16[128,1024]{1,0:T(8,128)(2,1)S(1)}, u32[]{:S(2)}, u32[]{:S(2)}) collective-permute-start(bf16[128,1024]{1,0:T(8,128)(2,1)S(1)} %get-tuple-element.44), channel_id=1, source_target_pairs={{0,24},{1,25},{2,26},{3,27},{4,28},{5,29},{6,30},{7,31},{8,0},{9,1... | collective-permute-start | bytes 786440 | tf_op jit(solution)/shard_map/ppermute | solution.py:81
  59.7 4.2 %slice-start.2 = ((s8[6291456]{0:T(1024)(128)(4,1)}), s8[4194304]{0:T(1024)(128)(4,1)S(1)}, s32[]{:S(2)}) async-start(s8[6291456]{0:T(1024)(128)(4,1)} %bitcast.93), calls=%async_computation.4 | async-start | bytes 8388608
  59.7 4.2 %slice-start.3 = ((s8[6291456]{0:T(1024)(128)(4,1)}), s8[2097152]{0:T(1024)(128)(4,1)S(1)}, s32[]{:S(2)}) async-start(s8[6291456]{0:T(1024)(128)(4,1)} %bitcast.93), calls=%async_computation.5 | async-start | bytes 4194304
  64.8 3.3 %collective-permute-start.7 = (bf16[16,640]{1,0:T(8,128)(2,1)S(1)}, bf16[16,640]{1,0:T(8,128)(2,1)S(1)}, u32[]{:S(2)}, u32[]{:S(2)}) collective-permute-start(bf16[16,640]{1,0:T(8,128)(2,1)S(1)} %bitcast.110), channel_id=1, source_target_pairs={{0,1},{1,0},{2,3},{3,2},{4,5},{5,4},{6,7},{7,6},{8,9},{9,8},{10,11... | collective-permute-start | bytes 61448 | tf_op jit(solution)/shard_map/ppermute | solution.py:81
  68.2 4.1 %collective-permute-start.8 = (bf16[32,640]{1,0:T(8,128)(2,1)S(1)}, bf16[32,640]{1,0:T(8,128)(2,1)S(1)}, u32[]{:S(2)}, u32[]{:S(2)}) collective-permute-start(bf16[32,640]{1,0:T(8,128)(2,1)S(1)} %get-tuple-element.62), channel_id=1, source_target_pairs={{0,2},{1,3},{2,4},{3,5},{4,6},{5,7},{6,0},{7,1},{8,10},{9,11},{10,... | collective-permute-start | bytes 122888 | tf_op jit(solution)/shard_map/ppermute | solution.py:81
  68.4 5.3 %collective-permute-start.9 = (bf16[32,640]{1,0:T(8,128)(2,1)S(1)}, bf16[32,640]{1,0:T(8,128)(2,1)S(1)}, u32[]{:S(2)}, u32[]{:S(2)}) collective-permute-start(bf16[32,640]{1,0:T(8,128)(2,1)S(1)} %get-tuple-element.62), channel_id=1, source_target_pairs={{0,4},{1,5},{2,6},{3,7},{4,0},{5,1},{6,2},{7,3},{8,12},{9,13},{10,... | collective-permute-start | bytes 122888 | tf_op jit(solution)/shard_map/ppermute | solution.py:81
  71.7 3.0 %collective-permute-start.10 = (bf16[32,640]{1,0:T(8,128)(2,1)S(1)}, bf16[32,640]{1,0:T(8,128)(2,1)S(1)}, u32[]{:S(2)}, u32[]{:S(2)}) collective-permute-start(bf16[32,640]{1,0:T(8,128)(2,1)S(1)} %get-tuple-element.62), channel_id=1, source_target_pairs={{0,6},{1,7},{2,0},{3,1},{4,2},{5,3},{6,4},{7,5},{8,14},{9,15},{10,... | collective-permute-start | bytes 122888 | tf_op jit(solution)/shard_map/ppermute | solution.py:81
  74.7 7.1 %collective-permute-start.11 = (bf16[128,640]{1,0:T(8,128)(2,1)S(1)}, bf16[128,640]{1,0:T(8,128)(2,1)S(1)}, u32[]{:S(2)}, u32[]{:S(2)}) collective-permute-start(bf16[128,640]{1,0:T(8,128)(2,1)S(1)} %get-tuple-element.50), channel_id=1, source_target_pairs={{0,8},{1,9},{2,10},{3,11},{4,12},{5,13},{6,14},{7,15},{8,16},{9,17... | collective-permute-start | bytes 491528 | tf_op jit(solution)/shard_map/ppermute | solution.py:81
  75.8 7.8 %collective-permute-start.12 = (bf16[128,640]{1,0:T(8,128)(2,1)S(1)}, bf16[128,640]{1,0:T(8,128)(2,1)S(1)}, u32[]{:S(2)}, u32[]{:S(2)}) collective-permute-start(bf16[128,640]{1,0:T(8,128)(2,1)S(1)} %get-tuple-element.50), channel_id=1, source_target_pairs={{0,16},{1,17},{2,18},{3,19},{4,20},{5,21},{6,22},{7,23},{8,24},{9,... | collective-permute-start | bytes 491528 | tf_op jit(solution)/shard_map/ppermute | solution.py:81
  80.8 4.5 %collective-permute-start.13 = (bf16[128,640]{1,0:T(8,128)(2,1)S(1)}, bf16[128,640]{1,0:T(8,128)(2,1)S(1)}, u32[]{:S(2)}, u32[]{:S(2)}) collective-permute-start(bf16[128,640]{1,0:T(8,128)(2,1)S(1)} %get-tuple-element.50), channel_id=1, source_target_pairs={{0,24},{1,25},{2,26},{3,27},{4,28},{5,29},{6,30},{7,31},{8,0},{9,1... | collective-permute-start | bytes 491528 | tf_op jit(solution)/shard_map/ppermute | solution.py:81
  86.6 8.4 %slice-start = ((s8[6553600]{0:T(1024)(128)(4,1)}), s8[2359296]{0:T(1024)(128)(4,1)S(1)}, s32[]{:S(2)}) async-start(s8[6553600]{0:T(1024)(128)(4,1)} %bitcast.91), calls=%async_computation.2 | async-start | bytes 4718592
  91.2 4.5 %slice-start.1 = ((s8[6553600]{0:T(1024)(128)(4,1)}), s8[4194304]{0:T(1024)(128)(4,1)S(1)}, s32[]{:S(2)}) async-start(s8[6553600]{0:T(1024)(128)(4,1)} %bitcast.91), calls=%async_computation.3 | async-start | bytes 8388608
  98.0 5.2 %copy-start.5 = (f32[256,64]{1,0:T(8,128)S(1)}, f32[256,64]{1,0:T(8,128)}, u32[]{:S(2)}) copy-start(f32[256,64]{1,0:T(8,128)} %get-tuple-element.71) | copy-start | bytes 196612
  98.9 5.8 %copy-start.2 = (pred[256,2560]{1,0:T(8,128)(4,1)S(1)}, pred[256,2560]{1,0:T(8,128)(4,1)}, u32[]{:S(2)}) copy-start(pred[256,2560]{1,0:T(8,128)(4,1)} %compare_and_fusion) | copy-start | bytes 1966084
  99.0 12.9 %copy-start.6 = (bf16[2,256,128]{2,1,0:T(8,128)(2,1)}, bf16[2,256,128]{2,1,0:T(8,128)(2,1)S(1)}, u32[]{:S(2)}) copy-start(bf16[2,256,128]{2,1,0:T(8,128)(2,1)S(1)} %pad_maximum_fusion.3) | copy-start | bytes 393220
  99.0 4.5 %collective-permute-start.15 = (bf16[2,256,128]{2,1,0:T(8,128)(2,1)S(1)}, bf16[2,256,128]{2,1,0:T(8,128)(2,1)}, u32[]{:S(2)}, u32[]{:S(2)}) collective-permute-start(bf16[2,256,128]{2,1,0:T(8,128)(2,1)S(1)} %pad_maximum_fusion.3), channel_id=1, source_target_pairs={{0,1},{1,0},{2,3},{3,2},{4,5},{5,4},{6,7},{7,6},{8,9},{9,8},{10,11... | collective-permute-start | bytes 393224 | tf_op jit(solution)/shard_map/ppermute | solution.py:16
  111.9 8.5 %copy-start.3 = (bf16[2,2048,128]{2,1,0:T(8,128)(2,1)S(1)}, bf16[2,2048,128]{2,1,0:T(8,128)(2,1)}, u32[]{:S(2)}) copy-start(bf16[2,2048,128]{2,1,0:T(8,128)(2,1)} %maximum_select_fusion) | copy-start | bytes 3145732
  (3 other events, 10.4 us)
